TPU v7x, 256 devices: a whole 4x4x8 slice. The times are simulated.
256 devices in a mesh: row: 16 (over z, core), col: 16 (over x, y).
Axes of the slice: x: 4, y: 4, z: 8, core: 2. Of those that a mesh axis runs over, the one named last changes fastest.
Arguments:
- site_tensor: bfloat16 [1024, 4, 1024], P('row', None, 'col'), may hold values from -180 to 180
- site_tangent: bfloat16 [1024, 4, 1024], P('row', None, 'col'), may hold values from -180 to 180
- left_env: bfloat16 [1024, 16384], P('row', 'col'), may hold values from -0.1875 to 0.375
- right_env: bfloat16 [1024, 16384], P('row', 'col'), may hold values from -0.046875 to 0.09375
- mpo: bfloat16 [16, 16, 4, 4], replicated, may hold values from -0.25 to 0.75
- dissipation: float32 [4], replicated, may hold values from 0.2 to 2
Outputs:
- evolved: float32 [1024, 4, 1024], P('row', None, 'col')
- evolved_tangent: float32 [1024, 4, 1024], P('row', None, 'col')
All inputs are finite; a program needn't handle non-finite values.
Results may differ from a plain program's by a relative error of at most 0.0055.
Values may be sent and summed in bfloat16 or wider, within the bound.
No kernel may reach another device: no remote copies, remote signals or barrier semaphores. Data moves between devices by JAX's collectives and lax.ppermute only.
A program may use at most 64 MiB of HBM per device.

v0:
```python
import jax
import jax.numpy as jnp
from jax import lax
from jax.sharding import PartitionSpec as P

KRYLOV = 3
taylor_order = 16


def inner(first, second):
    return jnp.sum(first * second)


def total(values):
    return lax.psum(lax.psum(values, "col"), "row")


def taylor(hess, dhess):
    size = hess.shape[0]
    term = jnp.zeros((size,), jnp.float32).at[0].set(1.0)
    dterm = jnp.zeros((size,), jnp.float32)
    total = term
    dtotal = dterm
    for order in range(1, taylor_order + 1):
        nterm = jnp.dot(hess, term, precision=lax.Precision.HIGHEST) / order
        dterm = (
            jnp.dot(dhess, term, precision=lax.Precision.HIGHEST)
            + jnp.dot(hess, dterm, precision=lax.Precision.HIGHEST)
        ) / order
        term = nterm
        total = total + term
        dtotal = dtotal + dterm
    return (total, dtotal)


def local(site_tensor, site_tangent, left_env, right_env, mpo, dissipation):
    rows_here, physical, cols_here = site_tensor.shape
    channels = mpo.shape[0]
    left_whole = lax.all_gather(left_env, "col", axis=1, tiled=True)
    right_whole = lax.all_gather(right_env, "row", axis=0, tiled=True)

    def apply(stacked):
        panels = stacked.shape[1]
        whole = lax.all_gather(stacked.astype(jnp.bfloat16), "row", axis=0, tiled=True)
        flat = whole.reshape(whole.shape[0], panels * physical * cols_here)
        left_three = left_whole.reshape(rows_here, flat.shape[0], channels)
        mixed = lax.dot_general(
            left_three, flat, (((1,), (0,)), ((), ())), preferred_element_type=jnp.float32
        )
        mixed = mixed.astype(jnp.bfloat16).reshape(rows_here, channels, panels, physical, cols_here)
        channel = jnp.einsum("awspr,wvpq->asqrv", mixed, mpo, preferred_element_type=jnp.float32)
        channel = channel.astype(jnp.bfloat16).reshape(
            rows_here * panels * physical, cols_here * channels
        )
        partial_rows = lax.dot_general(
            channel, right_whole, (((1,), (1,)), ((), ())), preferred_element_type=jnp.float32
        )
        partial_rows = partial_rows.reshape(rows_here, panels, physical, partial_rows.shape[1])
        summed = lax.psum_scatter(partial_rows, "col", scatter_dimension=3, tiled=True)
        return summed - dissipation[None, None, :, None] * stacked

    primal = site_tensor.astype(jnp.float32)
    tangent = site_tangent.astype(jnp.float32)
    starting = total(jnp.stack([inner(primal, primal), inner(primal, tangent)]))
    norm_site = jnp.sqrt(starting[0])
    norm_tangent = starting[1] / norm_site
    basis = [primal / norm_site]
    tangents = [(tangent - basis[0] * norm_tangent) / norm_site]
    hess = jnp.zeros((KRYLOV, KRYLOV), jnp.float32)
    dhess = jnp.zeros((KRYLOV, KRYLOV), jnp.float32)
    gram = jnp.zeros((KRYLOV, KRYLOV), jnp.float32)
    cross = jnp.zeros((KRYLOV, KRYLOV), jnp.float32)
    for level in range(KRYLOV):
        both = apply(jnp.stack([basis[level], tangents[level]], axis=1))
        image = both[:, 0]
        dimage = both[:, 1]
        counted = level + 1
        locals_list = [inner(vector, image) for vector in basis]
        locals_list = locals_list + [inner(vector, image) for vector in tangents]
        locals_list = locals_list + [inner(vector, dimage) for vector in basis]
        last = level + 1 == KRYLOV
        if not last:
            newest = basis[level]
            locals_list = locals_list + [inner(image, image), inner(image, dimage)]
            locals_list = locals_list + [inner(newest, vector) for vector in basis]
            locals_list = locals_list + [inner(newest, vector) for vector in tangents]
            locals_list = locals_list + [inner(vector, tangents[level]) for vector in basis[:level]]
        totals = total(jnp.stack(locals_list))
        coeffs = totals[:counted]
        across = totals[counted : 2 * counted]
        along = totals[2 * counted : 3 * counted]
        dcoeffs = across + along
        hess = hess.at[:counted, level].set(coeffs)
        dhess = dhess.at[:counted, level].set(dcoeffs)
        if not last:
            at = 3 * counted
            squared_image = totals[at]
            image_dimage = totals[at + 1]
            at += 2
            gram = gram.at[level, :counted].set(totals[at : at + counted])
            gram = gram.at[:counted, level].set(totals[at : at + counted])
            at += counted
            cross = cross.at[level, :counted].set(totals[at : at + counted])
            at += counted
            cross = cross.at[:level, level].set(totals[at : at + level])
            g = gram[:counted, :counted]
            t = cross[:counted, :counted]
            squared = (
                squared_image
                - 2.0 * jnp.sum(coeffs * coeffs)
                + jnp.dot(
                    coeffs,
                    jnp.dot(g, coeffs, precision=lax.Precision.HIGHEST),
                    precision=lax.Precision.HIGHEST,
                )
            )
            mixed_term = (
                image_dimage
                - jnp.sum(dcoeffs * coeffs)
                - jnp.sum(coeffs * across)
                - jnp.sum(coeffs * along)
                + jnp.dot(
                    coeffs,
                    jnp.dot(g, dcoeffs, precision=lax.Precision.HIGHEST),
                    precision=lax.Precision.HIGHEST,
                )
                + jnp.dot(
                    coeffs,
                    jnp.dot(t, coeffs, precision=lax.Precision.HIGHEST),
                    precision=lax.Precision.HIGHEST,
                )
            )
            residual = image
            dresidual = dimage
            for index in range(counted):
                residual = residual - coeffs[index] * basis[index]
                dresidual = (
                    dresidual - dcoeffs[index] * basis[index] - coeffs[index] * tangents[index]
                )
            height = jnp.sqrt(squared)
            dheight = mixed_term / height
            newvec = residual / height
            basis.append(newvec)
            tangents.append((dresidual - newvec * dheight) / height)
            hess = hess.at[level + 1, level].set(height)
            dhess = dhess.at[level + 1, level].set(dheight)
    coeff, dcoeff = taylor(hess, dhess)
    spread = jnp.zeros_like(primal)
    dspread = jnp.zeros_like(primal)
    for index in range(KRYLOV):
        spread = spread + coeff[index] * basis[index]
        dspread = dspread + coeff[index] * tangents[index] + dcoeff[index] * basis[index]
    evolved = norm_site * spread
    evolved_tangent = norm_tangent * spread + norm_site * dspread
    return (evolved, evolved_tangent)


def solution(mesh):
    in_specs = (
        P("row", None, "col"),
        P("row", None, "col"),
        P("row", "col"),
        P("row", "col"),
        P(),
        P(),
    )
    out_specs = (P("row", None, "col"), P("row", None, "col"))
    return jax.shard_map(local, mesh=mesh, in_specs=in_specs, out_specs=out_specs, check_vma=False)
```

profile of v0, /device:TPU:1, one launch (start us, length us, event | category | flops | bytes accessed | tf_op | source)
XLA Modules:
  0.0 870.2 jit_solution(10881828648179970118)
XLA Ops:
  10.1 34.2 %psum.56 = f32[2]{0:T(128)S(1)} all-reduce(f32[2]{0:T(128)S(1)} %pad_maximum_fusion.3), channel_id=1, replica_groups=mesh['row'=16,'col'=16] {'col'}, use_global_device_ids=true, to_apply=%region_2.0 | all-reduce | flops 2 | bytes 16 | tf_op jit(solution)/shard_map/psum | solution.py:15
  44.3 33.8 %psum.57 = f32[2]{0:T(128)S(1)} all-reduce(f32[2]{0:T(128)S(1)} %psum.56), channel_id=1, replica_groups=mesh['row'=16,'col'=16] {'row'}, use_global_device_ids=true, to_apply=%region_3.0 | all-reduce | flops 2 | bytes 16 | tf_op jit(solution)/shard_map/psum | solution.py:15
  84.3 32.3 %all-gather.6.cloned.1.call-done = bf16[1024,2,4,64]{3,2,1,0:T(4,128)(2,1)} async-done(((bf16[64,2,4,64]{3,2,1,0:T(4,128)(2,1)}), bf16[1024,2,4,64]{3,2,1,0:T(4,128)(2,1)}) %all-gather.6.cloned.1.call-update) | async-done | bytes 1048592 | tf_op jit(solution)/shard_map/all_gather | solution.py:44
  120.7 44.7 %all-gather.8.cloned.1.call-done = bf16[64,16384]{1,0:T(8,128)(2,1)} async-done(((bf16[64,1024]{1,0:T(8,128)(2,1)}), bf16[64,16384]{1,0:T(8,128)(2,1)}) %all-gather.8.cloned.1.call-update) | async-done | bytes 2097168 | tf_op jit(solution)/shard_map/all_gather | solution.py:39
  187.6 5.8 copy.115
  193.4 14.8 %all-gather.10.cloned.1.call-done = bf16[1024,1024]{1,0:T(8,128)(2,1)} async-done(((bf16[64,1024]{1,0:T(8,128)(2,1)}), bf16[1024,1024]{1,0:T(8,128)(2,1)}) %all-gather.10.cloned.1.call-update) | async-done | bytes 2097168 | tf_op jit(solution)/shard_map/all_gather | solution.py:40
  208.1 6.0 fusion.5
  225.0 76.2 %reduce-scatter.10.cloned.1.call-done = f32[64,512]{1,0:T(8,128)} async-done(((f32[1024,512]{1,0:T(8,128)}), f32[64,512]{1,0:T(8,128)}) %reduce-scatter.10.cloned.1.call-update) | async-done | bytes 131088
  307.8 30.9 %psum.58 = f32[7]{0:T(128)S(1)} all-reduce(f32[7]{0:T(128)S(1)} %stack.145), channel_id=1, replica_groups=mesh['row'=16,'col'=16] {'col'}, use_global_device_ids=true, to_apply=%region_12.0 | all-reduce | flops 7 | bytes 56 | tf_op jit(solution)/shard_map/psum | solution.py:15
  338.7 32.9 %psum.59 = f32[7]{0:T(128)S(1)} all-reduce(f32[7]{0:T(128)S(1)} %psum.58), channel_id=1, replica_groups=mesh['row'=16,'col'=16] {'row'}, use_global_device_ids=true, to_apply=%region_13.0 | all-reduce | flops 7 | bytes 56 | tf_op jit(solution)/shard_map/psum | solution.py:15
  384.9 35.9 %all-gather.12.cloned.1.call-done = bf16[1024,2,4,64]{3,2,1,0:T(4,128)(2,1)} async-done(((bf16[64,2,4,64]{3,2,1,0:T(4,128)(2,1)}), bf16[1024,2,4,64]{3,2,1,0:T(4,128)(2,1)}) %all-gather.12.cloned.1.call-update) | async-done | bytes 1048592 | tf_op jit(solution)/shard_map/all_gather | solution.py:44
  437.7 5.8 copy.123
  443.5 6.0 fusion.3
  462.4 74.2 %reduce-scatter.12.cloned.1.call-done = f32[64,512]{1,0:T(8,128)} async-done(((f32[1024,512]{1,0:T(8,128)}), f32[64,512]{1,0:T(8,128)}) %reduce-scatter.12.cloned.1.call-update) | async-done | bytes 131088
  538.8 8.2 stack.162
  547.7 30.9 %psum.60 = f32[13]{0:T(128)S(1)} all-reduce(f32[13]{0:T(128)S(1)} %stack.162), channel_id=1, replica_groups=mesh['row'=16,'col'=16] {'col'}, use_global_device_ids=true, to_apply=%region_28.0 | all-reduce | flops 13 | bytes 104 | tf_op jit(solution)/shard_map/psum | solution.py:15
  578.6 33.1 %psum.61 = f32[13]{0:T(128)S(1)} all-reduce(f32[13]{0:T(128)S(1)} %psum.60), channel_id=1, replica_groups=mesh['row'=16,'col'=16] {'row'}, use_global_device_ids=true, to_apply=%region_29.0 | all-reduce | flops 13 | bytes 104 | tf_op jit(solution)/shard_map/psum | solution.py:15
  631.7 35.9 %all-gather.14.cloned.1.call-done = bf16[1024,2,4,64]{3,2,1,0:T(4,128)(2,1)} async-done(((bf16[64,2,4,64]{3,2,1,0:T(4,128)(2,1)}), bf16[1024,2,4,64]{3,2,1,0:T(4,128)(2,1)}) %all-gather.14.cloned.1.call-update) | async-done | bytes 1048592 | tf_op jit(solution)/shard_map/all_gather | solution.py:44
  681.8 5.8 copy.132
  695.5 5.6 reshape.689
  704.9 73.0 %reduce-scatter.14.cloned.1.call-done = f32[64,512]{1,0:T(8,128)} async-done(((f32[1024,512]{1,0:T(8,128)}), f32[64,512]{1,0:T(8,128)}) %reduce-scatter.14.cloned.1.call-update) | async-done | bytes 131088
  780.0 5.7 stack.175
  785.9 30.9 %psum.62 = f32[9]{0:T(128)S(1)} all-reduce(f32[9]{0:T(128)S(1)} %stack.175), channel_id=1, replica_groups=mesh['row'=16,'col'=16] {'col'}, use_global_device_ids=true, to_apply=%region_45.0 | all-reduce | flops 9 | bytes 72 | tf_op jit(solution)/shard_map/psum | solution.py:15
  816.9 32.9 %psum.63 = f32[9]{0:T(128)S(1)} all-reduce(f32[9]{0:T(128)S(1)} %psum.62), channel_id=1, replica_groups=mesh['row'=16,'col'=16] {'row'}, use_global_device_ids=true, to_apply=%region_46.0 | all-reduce | flops 9 | bytes 72 | tf_op jit(solution)/shard_map/psum | solution.py:15
  (154 shorter events, 140.4 us)
Async XLA Ops:
  7.2 109.4 %all-gather.6.cloned.1.call-start = ((), (), s32[]{:S(2)}) async-start(), calls=%async_computation.3 | async-start | bytes 2228224 | tf_op jit(solution)/shard_map/all_gather | solution.py:44
  81.8 83.7 %all-gather.8.cloned.1.call-start = ((), (), s32[]{:S(2)}) async-start(), calls=%async_computation.4 | async-start | bytes 2228224 | tf_op jit(solution)/shard_map/all_gather | solution.py:39
  82.5 125.6 %all-gather.10.cloned.1.call-start = ((), (), s32[]{:S(2)}) async-start(), calls=%async_computation.5 | async-start | bytes 2228224 | tf_op jit(solution)/shard_map/all_gather | solution.py:40
  83.3 218.0 %reduce-scatter.10.cloned.1.call-start = ((), (), s32[]{:S(2)}) async-start(), calls=%async_computation.8 | async-start | bytes 2228224
  224.5 78.0 %copy-start.2 = (f32[4]{0:T(128)S(1)}, f32[4]{0:T(128)}, u32[]{:S(2)}) copy-start(f32[4]{0:T(128)} %param.47) | copy-start | bytes 52
  224.5 78.1 %copy-start = (bf16[64,4,64]{2,1,0:T(4,128)(2,1)S(1)}, bf16[64,4,64]{2,1,0:T(4,128)(2,1)}, u32[]{:S(2)}) copy-start(bf16[64,4,64]{2,1,0:T(4,128)(2,1)} %param.42) | copy-start | bytes 98308
  224.5 78.1 %copy-start.1 = (bf16[64,4,64]{2,1,0:T(4,128)(2,1)S(1)}, bf16[64,4,64]{2,1,0:T(4,128)(2,1)}, u32[]{:S(2)}) copy-start(bf16[64,4,64]{2,1,0:T(4,128)(2,1)} %param.43) | copy-start | bytes 98308
  224.5 196.3 %all-gather.12.cloned.1.call-start = ((), (), s32[]{:S(2)}) async-start(), calls=%async_computation.6 | async-start | bytes 2228224 | tf_op jit(solution)/shard_map/all_gather | solution.py:44
  384.8 151.8 %reduce-scatter.12.cloned.1.call-start = ((), (), s32[]{:S(2)}) async-start(), calls=%async_computation.9 | async-start | bytes 2228224
  459.9 207.7 %all-gather.14.cloned.1.call-start = ((), (), s32[]{:S(2)}) async-start(), calls=%async_computation.7 | async-start | bytes 2228224 | tf_op jit(solution)/shard_map/all_gather | solution.py:44
  631.7 146.2 %reduce-scatter.14.cloned.1.call-start = ((), (), s32[]{:S(2)}) async-start(), calls=%async_computation.10 | async-start | bytes 2228224
  701.1 148.9 %copy-start.3 = (f32[3,1]{0,1:T(1,128)S(1)}, f32[3,1]{0,1:T(1,128)}, u32[]{:S(2)}) copy-start(f32[3,1]{0,1:T(1,128)} %constant.468) | copy-start | bytes 40
Sparse Core Ops, SparseCore 0:
  81.9 34.6 all-gather.5
  119.1 46.3 all-gather.7
  167.3 40.7 all-gather.9
  224.6 76.5 reduce-scatter.9
  385.0 35.7 all-gather.11
  460.0 76.5 reduce-scatter.11
  631.8 35.7 all-gather.13
  701.2 76.6 reduce-scatter.13
where the time goes:
time: 881 us; the launch traced here: 870 us
  waiting for transfers between devices  388 us (44%)
  blocking collectives  260 us (30%)
  local copies, waits for them, and re-layouts  123 us (14%)
  matrix products  48.2 us (5%)
  between operations  34.5 us (4%)
  other arithmetic  15.4 us (2%)
    psum x8, blocking collectives, total(): return lax.psum(lax.psum(values, 'col'), 'row')  260 us
    unnamed x11, waiting for transfers between devices  225 us
    all_gather x3, waiting for transfers between devices, apply(): lax.all_gather(stacked.astype(jnp.bfloat16), 'row', axis=0, tiled=True)  104 us
    all_gather x1, waiting for transfers between devices, local(): left_whole = lax.all_gather(left_env, 'col', axis=1, tiled=True)  44.7 us
    unnamed x23, local copies, waits for them, and re-layouts  35.7 us
    another operation x3, local copies, waits for them, and re-layouts, local(): totals = total(jnp.stack(locals_list))  18.4 us
  transfers between devices with their start and end apart: 8, of which 8 were waited for; matrix products, arithmetic and copies ran while one was open for 5% of the time, Pallas kernels for 0%

commit v1 on v0

--- a/solution.py
+++ b/solution.py
@@ -5,6 +5,22 @@
 
 KRYLOV = 3
 taylor_order = 16
+
+
+def gather_around(x, axis, dim):
+    ways, here, step = (lax.axis_size(axis), lax.axis_index(axis), x.shape[dim])
+    shape = [n * ways if d == dim else n for d, n in enumerate(x.shape)]
+    full = lax.dynamic_update_slice_in_dim(jnp.zeros(shape, x.dtype), x, here * step, axis=dim)
+    going_up = going_down = x
+    for far in range(1, ways // 2 + 1):
+        going_up = lax.ppermute(going_up, axis, [(d, (d + 1) % ways) for d in range(ways)])
+        full = lax.dynamic_update_slice_in_dim(full, going_up, (here - far) % ways * step, axis=dim)
+        if 2 * far < ways:
+            going_down = lax.ppermute(going_down, axis, [(d, (d - 1) % ways) for d in range(ways)])
+            full = lax.dynamic_update_slice_in_dim(
+                full, going_down, (here + far) % ways * step, axis=dim
+            )
+    return full
 
 
 def inner(first, second):
@@ -36,7 +52,7 @@
 def local(site_tensor, site_tangent, left_env, right_env, mpo, dissipation):
     rows_here, physical, cols_here = site_tensor.shape
     channels = mpo.shape[0]
-    left_whole = lax.all_gather(left_env, "col", axis=1, tiled=True)
+    left_whole = gather_around(left_env, "col", 1)
     right_whole = lax.all_gather(right_env, "row", axis=0, tiled=True)
 
     def apply(stacked):

time: 881 us -> 848 us (0.963)
  waiting for transfers between devices: 388 us -> 313 us
  starting transfers between devices: 0.79 us -> 35.5 us
  local copies, waits for them, and re-layouts: 123 us -> 135 us
    all_gather x1 -> x0, waiting for transfers between devices: 44.7 us -> none  [local(): left_whole = lax.all_gather(left_env, 'col', axis=1, tiled=True)]
    ppermute x0 -> x15, starting transfers between devices: none -> 34.9 us  [the longest x7 33.8 us: gather_around(): lax.ppermute(going_down, axis, [(d, (d - 1) % ways) for d in range(ways)])]
    all_gather x3, waiting for transfers between devices: 104 us -> 71.4 us  [apply(): lax.all_gather(stacked.astype(jnp.bfloat16), 'row', axis=0, tiled=True)]
    all_gather x1, waiting for transfers between devices: 14.8 us -> 0.01 us  [local(): right_whole = lax.all_gather(right_env, 'row', axis=0, tiled=True)]
    dynamic_update_slice x0 -> x16, local copies, waits for them, and re-layouts: none -> 11.7 us  [the longest x8 5.87 us: gather_around(): lax.dynamic_update_slice_in_dim(full, going_up, (here - far) % ways * ste...]
    ppermute x0 -> x15, waiting for transfers between devices: none -> 10.5 us  [the longest x8 10.5 us: gather_around(): lax.ppermute(going_up, axis, [(d, (d + 1) % ways) for d in range(ways)])]
    unnamed x11 -> x10, waiting for transfers between devices: 225 us -> 232 us
    unnamed x23 -> x30, local copies, waits for them, and re-layouts: 35.7 us -> 36.6 us
  transfers between devices with their start and end apart: 8 -> 22, of which waited for: 8 -> 12; matrix products, arithmetic and copies ran while one was open for 5% -> 6% of each run, Pallas kernels for 0% -> 0%
where the time goes in v1:
time: 848 us; the launch traced here: 837 us
  waiting for transfers between devices  313 us (37%)
  blocking collectives  259 us (31%)
  local copies, waits for them, and re-layouts  135 us (16%)
  matrix products  42.7 us (5%)
  between operations  35.8 us (4%)
  starting transfers between devices  35.5 us (4%)
  other arithmetic  15.4 us (2%)
    psum x8, blocking collectives, total(): return lax.psum(lax.psum(values, 'col'), 'row')  259 us
    unnamed x10, waiting for transfers between devices  232 us
    all_gather x3, waiting for transfers between devices, apply(): lax.all_gather(stacked.astype(jnp.bfloat16), 'row', axis=0, tiled=True)  71.4 us
    unnamed x30, local copies, waits for them, and re-layouts  36.6 us
    ppermute x7, starting transfers between devices, gather_around(): lax.ppermute(going_down, axis, [(d, (d - 1) % ways) for d in range(ways)])  33.8 us
    another operation x3, local copies, waits for them, and re-layouts, local(): totals = total(jnp.stack(locals_list))  18.3 us
    convert_element_type x3, local copies, waits for them, and re-layouts, apply(): channel.astype(jnp.bfloat16)  17.4 us
  transfers between devices with their start and end apart: 22, of which 12 were waited for; matrix products, arithmetic and copies ran while one was open for 6% of the time, Pallas kernels for 0%

profile of v1, /device:TPU:1, one launch (start us, length us, event | category | flops | bytes accessed | tf_op | source)
XLA Modules:
  0.0 837.0 jit_solution(18180790587305785814)
XLA Ops:
  10.1 34.2 %psum.56 = f32[2]{0:T(128)S(1)} all-reduce(f32[2]{0:T(128)S(1)} %pad_maximum_fusion.3), channel_id=1, replica_groups=mesh['row'=16,'col'=16] {'col'}, use_global_device_ids=true, to_apply=%region_2.3 | all-reduce | flops 2 | bytes 16 | tf_op jit(solution)/shard_map/psum | solution.py:31
  44.3 33.8 %psum.57 = f32[2]{0:T(128)S(1)} all-reduce(f32[2]{0:T(128)S(1)} %psum.56), channel_id=1, replica_groups=mesh['row'=16,'col'=16] {'row'}, use_global_device_ids=true, to_apply=%region_3.4 | all-reduce | flops 2 | bytes 16 | tf_op jit(solution)/shard_map/psum | solution.py:31
  139.4 6.1 collective-permute-done.14
  146.4 5.8 copy.171
  165.9 5.8 copy.175
  171.7 6.0 fusion.5
  182.4 5.6 reshape.685
  188.1 82.4 %reduce-scatter.10.cloned.1.call-done = f32[64,512]{1,0:T(8,128)} async-done(((f32[1024,512]{1,0:T(8,128)}), f32[64,512]{1,0:T(8,128)}) %reduce-scatter.10.cloned.1.call-update) | async-done | bytes 131088
  277.1 30.9 %psum.58 = f32[7]{0:T(128)S(1)} all-reduce(f32[7]{0:T(128)S(1)} %stack.145), channel_id=1, replica_groups=mesh['row'=16,'col'=16] {'col'}, use_global_device_ids=true, to_apply=%region_12.13 | all-reduce | flops 7 | bytes 56 | tf_op jit(solution)/shard_map/psum | solution.py:31
  308.0 32.9 %psum.59 = f32[7]{0:T(128)S(1)} all-reduce(f32[7]{0:T(128)S(1)} %psum.58), channel_id=1, replica_groups=mesh['row'=16,'col'=16] {'row'}, use_global_device_ids=true, to_apply=%region_13.14 | all-reduce | flops 7 | bytes 56 | tf_op jit(solution)/shard_map/psum | solution.py:31
  355.2 35.7 %all-gather.9.cloned.1.call-done = bf16[1024,2,4,64]{3,2,1,0:T(4,128)(2,1)} async-done(((bf16[64,2,4,64]{3,2,1,0:T(4,128)(2,1)}), bf16[1024,2,4,64]{3,2,1,0:T(4,128)(2,1)}) %all-gather.9.cloned.1.call-update) | async-done | bytes 1048592 | tf_op jit(solution)/shard_map/all_gather | solution.py:60
  404.5 5.8 copy.183
  410.3 6.0 fusion.3
  429.4 74.0 %reduce-scatter.12.cloned.1.call-done = f32[64,512]{1,0:T(8,128)} async-done(((f32[1024,512]{1,0:T(8,128)}), f32[64,512]{1,0:T(8,128)}) %reduce-scatter.12.cloned.1.call-update) | async-done | bytes 131088
  505.5 8.2 stack.162
  514.4 30.9 %psum.60 = f32[13]{0:T(128)S(1)} all-reduce(f32[13]{0:T(128)S(1)} %stack.162), channel_id=1, replica_groups=mesh['row'=16,'col'=16] {'col'}, use_global_device_ids=true, to_apply=%region_28.29 | all-reduce | flops 13 | bytes 104 | tf_op jit(solution)/shard_map/psum | solution.py:31
  545.3 32.9 %psum.61 = f32[13]{0:T(128)S(1)} all-reduce(f32[13]{0:T(128)S(1)} %psum.60), channel_id=1, replica_groups=mesh['row'=16,'col'=16] {'row'}, use_global_device_ids=true, to_apply=%region_29.30 | all-reduce | flops 13 | bytes 104 | tf_op jit(solution)/shard_map/psum | solution.py:31
  598.5 35.7 %all-gather.11.cloned.1.call-done = bf16[1024,2,4,64]{3,2,1,0:T(4,128)(2,1)} async-done(((bf16[64,2,4,64]{3,2,1,0:T(4,128)(2,1)}), bf16[1024,2,4,64]{3,2,1,0:T(4,128)(2,1)}) %all-gather.11.cloned.1.call-update) | async-done | bytes 1048592 | tf_op jit(solution)/shard_map/all_gather | solution.py:60
  647.4 5.8 copy.192
  661.0 5.6 reshape.689
  669.0 74.3 %reduce-scatter.14.cloned.1.call-done = f32[64,512]{1,0:T(8,128)} async-done(((f32[1024,512]{1,0:T(8,128)}), f32[64,512]{1,0:T(8,128)}) %reduce-scatter.14.cloned.1.call-update) | async-done | bytes 131088
  745.4 5.7 stack.175
  752.4 30.9 %psum.62 = f32[9]{0:T(128)S(1)} all-reduce(f32[9]{0:T(128)S(1)} %stack.175), channel_id=1, replica_groups=mesh['row'=16,'col'=16] {'col'}, use_global_device_ids=true, to_apply=%region_45.46 | all-reduce | flops 9 | bytes 72 | tf_op jit(solution)/shard_map/psum | solution.py:31
  783.4 32.9 %psum.63 = f32[9]{0:T(128)S(1)} all-reduce(f32[9]{0:T(128)S(1)} %psum.62), channel_id=1, replica_groups=mesh['row'=16,'col'=16] {'row'}, use_global_device_ids=true, to_apply=%region_46.47 | all-reduce | flops 9 | bytes 72 | tf_op jit(solution)/shard_map/psum | solution.py:31
  (219 shorter events, 173.4 us)
Async XLA Ops:
  7.2 145.1 %all-gather.5.cloned.1.call-start = ((), (), s32[]{:S(2)}) async-start(), calls=%async_computation.3 | async-start | bytes 2228224 | tf_op jit(solution)/shard_map/all_gather | solution.py:60
  81.8 89.9 %all-gather.7.cloned.1.call-start = ((), (), s32[]{:S(2)}) async-start(), calls=%async_computation.4 | async-start | bytes 2228224 | tf_op jit(solution)/shard_map/all_gather | solution.py:56
  82.5 188.0 %reduce-scatter.10.cloned.1.call-start = ((), (), s32[]{:S(2)}) async-start(), calls=%async_computation.7 | async-start | bytes 2228224
  82.6 9.7 %collective-permute-start = (bf16[64,1024]{1,0:T(8,128)(2,1)}, bf16[64,1024]{1,0:T(8,128)(2,1)S(1)}, u32[]{:S(2)}, u32[]{:S(2)}) collective-permute-start(bf16[64,1024]{1,0:T(8,128)(2,1)} %param.44), channel_id=1, source_target_pairs={{0,1},{1,2},{2,3},{3,4},{4,5},{5,6},{6,7},{7,8},{8,9},{9,10},{10,1... | collective-permute-start | bytes 393224 | tf_op jit(solution)/shard_map/ppermute | solution.py:16
  82.7 10.6 %collective-permute-start.1 = (bf16[64,1024]{1,0:T(8,128)(2,1)}, bf16[64,1024]{1,0:T(8,128)(2,1)S(1)}, u32[]{:S(2)}, u32[]{:S(2)}) collective-permute-start(bf16[64,1024]{1,0:T(8,128)(2,1)} %param.44), channel_id=1, source_target_pairs={{0,15},{1,0},{2,1},{3,2},{4,3},{5,4},{6,5},{7,6},{8,7},{9,8},{10,9... | collective-permute-start | bytes 393224 | tf_op jit(solution)/shard_map/ppermute | solution.py:19
  92.5 7.8 collective-permute-start.2
  93.5 7.7 collective-permute-start.3
  100.4 7.2 collective-permute-start.4
  101.4 7.2 collective-permute-start.5
  107.8 7.2 collective-permute-start.6
  108.8 7.2 collective-permute-start.7
  115.2 7.2 collective-permute-start.8
  116.2 7.2 collective-permute-start.9
  122.6 7.2 collective-permute-start.10
  123.6 7.5 collective-permute-start.11
  129.9 7.6 collective-permute-start.12
  131.3 7.2 collective-permute-start.13
  137.7 7.8 collective-permute-start.14
  188.0 83.8 %copy-start.1 = (bf16[64,4,64]{2,1,0:T(4,128)(2,1)S(1)}, bf16[64,4,64]{2,1,0:T(4,128)(2,1)}, u32[]{:S(2)}) copy-start(bf16[64,4,64]{2,1,0:T(4,128)(2,1)} %param.43) | copy-start | bytes 98308
  188.1 202.9 %all-gather.9.cloned.1.call-start = ((), (), s32[]{:S(2)}) async-start(), calls=%async_computation.5 | async-start | bytes 2228224 | tf_op jit(solution)/shard_map/all_gather | solution.py:60
  355.0 148.3 %reduce-scatter.12.cloned.1.call-start = ((), (), s32[]{:S(2)}) async-start(), calls=%async_computation.8 | async-start | bytes 2228224
  426.7 207.5 %all-gather.11.cloned.1.call-start = ((), (), s32[]{:S(2)}) async-start(), calls=%async_computation.6 | async-start | bytes 2228224 | tf_op jit(solution)/shard_map/all_gather | solution.py:60
  598.3 145.1 %reduce-scatter.14.cloned.1.call-start = ((), (), s32[]{:S(2)}) async-start(), calls=%async_computation.9 | async-start | bytes 2228224
  666.6 150.0 %copy-start.6 = (f32[3,1]{0,1:T(1,128)S(1)}, f32[3,1]{0,1:T(1,128)}, u32[]{:S(2)}) copy-start(f32[3,1]{0,1:T(1,128)} %constant.576) | copy-start | bytes 40
  (5 other events, 179.9 us)
Sparse Core Ops, SparseCore 0:
  81.9 34.6 all-gather.4
  118.4 37.8 all-gather.6
  188.2 82.2 reduce-scatter.9
  355.1 35.7 all-gather.8
  426.8 76.4 reduce-scatter.11
  598.4 35.7 all-gather.10
  666.8 76.5 reduce-scatter.13
